TPU v7x, 32 devices: a whole 2x2x4 slice. The times are simulated.
32 devices in a mesh: groups: 2 (over y), prompt: 4 (over z), enc: 4 (over x, core).
Axes of the slice: x: 2, y: 2, z: 4, core: 2. Of those that a mesh axis runs over, the one named last changes fastest.
Arguments:
- embed: bfloat16 [8192, 256], P(('groups', 'prompt', 'enc')), parts along dimension 0, may hold values from -4000 to 4000
- coords: int32 [64, 6], P(('groups', 'prompt')), parts along dimension 0, may hold values from 0 to 1023
- targets: int32 [64], P(('groups', 'prompt')), parts along dimension 0, may hold values from 0 to 7
- counts: int32 [4], replicated, may hold values from 1 to 8, 16 in all
- labels: int32 [512, 256], P('groups'), parts along dimension 0, may hold values from 0 to 7
- type_embed: float32 [4, 256], replicated, may hold values from -5 to 5
- fourier: float32 [2, 128], replicated, may hold values from -5 to 5
- wq_t: bfloat16 [256, 128], replicated, may hold values from -0.375 to 0.375
- wk_t: bfloat16 [256, 128], replicated, may hold values from -0.375 to 0.375
- wv_t: bfloat16 [256, 128], replicated, may hold values from -0.375 to 0.375
- wo_t: bfloat16 [128, 256], replicated, may hold values from -0.5 to 0.5
- wq_i: bfloat16 [256, 128], replicated, may hold values from -0.375 to 0.375
- wk_i: bfloat16 [256, 128], replicated, may hold values from -0.375 to 0.375
- wv_i: bfloat16 [256, 128], replicated, may hold values from -0.375 to 0.375
- wo_i: bfloat16 [128, 256], replicated, may hold values from -0.5 to 0.5
- gain_one: float32 [256], replicated, may hold values from 0.1 to 1.9
- gain_two: float32 [256], replicated, may hold values from 0.1 to 1.9
- gain_three: float32 [64], replicated, may hold values from 0.1 to 1.9
- up_one: bfloat16 [256, 256], replicated, may hold values from -0.375 to 0.375
- second_upsample_weight: bfloat16 [64, 128], replicated, may hold values from -0.75 to 0.75
- hyper_one: bfloat16 [256, 256], replicated, may hold values from -0.375 to 0.375
- hyper_two: bfloat16 [256, 32], replicated, may hold values from -0.375 to 0.375
Outputs:
- grad_embed: float32 [8192, 256], P(('groups', 'prompt', 'enc')), parts along dimension 0
There are 2 independent parts, one for each index of `groups`. A program takes and returns all parts, laid end to end along the dimension named above; an argument that names none is the same for every part. Nothing has to cross between parts.
Inputs may be any that keep to these rules, and one draw needn't show every extreme that they name: Prompt index p has counts[p] live prompts, in its first slots; the counts sum to 16 and the largest is 8.
All inputs are finite; a program needn't handle non-finite values.
Results may differ from a plain program's by a relative error of at most 0.0035.
Values may be sent and summed in bfloat16 or wider, within the bound.
No kernel may reach another device: no remote copies, remote signals or barrier semaphores. Data moves between devices by JAX's collectives and lax.ppermute only.
A program may use at most 128 MiB of HBM per device.

v0:
```python
import math
import jax
import jax.numpy as jnp
from jax import lax
from jax.sharding import PartitionSpec as P

HEADS = 8
HD = 16
IMG = 1024
highest_value = lax.Precision.HIGHEST
epsilon = 1e-05


def joined(array, axis, combine):
    everything = jax.tree.map(lambda part: lax.all_gather(part, axis), array)
    leading = jax.tree.map(lambda part: part[0], everything)

    def step(k, so_far):
        return combine(so_far, jax.tree.map(lambda part: part[k], everything))

    return lax.fori_loop(1, lax.axis_size(axis), step, leading)


def layer_norm(values, gain):
    centered = values - jnp.mean(values, axis=-1, keepdims=True)
    variance = jnp.mean(centered * centered, axis=-1, keepdims=True)
    return centered * lax.rsqrt(variance + epsilon) * gain


def fourier_code(pixel_pair, fourier):
    scaled = 2.0 * ((pixel_pair.astype(jnp.float32) + 0.5) / IMG) - 1.0
    angles = 2.0 * math.pi * jnp.dot(scaled, fourier, precision=highest_value)
    return jnp.concatenate([jnp.sin(angles), jnp.cos(angles)], axis=-1)


def prompt_tokens(corner_rows, type_embed, fourier):
    point_code = fourier_code(corner_rows[..., 0:2], fourier) + type_embed[1]
    first_code = fourier_code(corner_rows[..., 2:4], fourier) + type_embed[2]
    second_code = fourier_code(corner_rows[..., 4:6], fourier) + type_embed[3]
    output_token = jnp.broadcast_to(type_embed[0], point_code.shape)
    return jnp.stack([output_token, point_code, first_code, second_code], axis=-2)


def token_pixel_scores(labels):
    side = labels.shape[0] // 4
    grid_view = labels.reshape(side, 2, 2, side, 2, 2)
    grid_view = jnp.transpose(grid_view, (0, 3, 1, 4, 2, 5))
    return grid_view.reshape(side * side, 4, 4)


def combine_parts(first, second_result):
    top_first, first_running_total, accum_first = first
    top_second, total_second, accum_second = second_result
    top_both = jnp.maximum(top_first, top_second)
    factor_first = jnp.exp(top_first - top_both)
    factor_second = jnp.exp(top_second - top_both)
    total_both = first_running_total * factor_first + total_second * factor_second
    accum_both = accum_first * factor_first[..., None] + accum_second * factor_second[..., None]
    return (top_both, total_both, accum_both)


def image_side(query_image, image_float, tokens_one, truth, live_flag, side_weights):
    wk_i, wv_i, wo_i, gain_two, up_one, gain_three, second_upsample_weight, hyper_one, hyper_two = (
        side_weights
    )
    head_scale = HD ** (-0.5)
    row_count = query_image.shape[0]
    token_keys = jnp.dot(tokens_one, wk_i.astype(jnp.float32), precision=highest_value).reshape(
        -1, HEADS, HD
    )
    token_values = jnp.dot(tokens_one, wv_i.astype(jnp.float32), precision=highest_value).reshape(
        -1, HEADS, HD
    )
    scores = (
        jnp.einsum(
            "jhd,rhd->jhr",
            query_image.reshape(row_count, HEADS, HD),
            token_keys,
            precision=highest_value,
        )
        * head_scale
    )
    attention = jax.nn.softmax(scores, axis=-1)
    mixed = (
        jnp.einsum("jhr,rhd->jhd", attention, token_values, precision=highest_value)
        .reshape(row_count, -1)
        .astype(jnp.bfloat16)
    )
    update = jnp.dot(mixed, wo_i, preferred_element_type=jnp.float32)
    image_one = layer_norm(image_float + update, gain_two).astype(jnp.bfloat16)
    lifted = jnp.dot(image_one, up_one, preferred_element_type=jnp.float32).reshape(
        row_count, 4, -1
    )
    first_activation = jax.nn.gelu(layer_norm(lifted, gain_three), approximate=False).astype(
        jnp.bfloat16
    )
    second_result = jnp.einsum(
        "oij,jp->oip", first_activation, second_upsample_weight, preferred_element_type=jnp.float32
    )
    features = jax.nn.gelu(second_result, approximate=False).reshape(row_count, 4, 4, -1)
    hidden = jax.nn.relu(
        jnp.dot(tokens_one[0], hyper_one.astype(jnp.float32), precision=highest_value)
    )
    hyper = jnp.dot(hidden, hyper_two.astype(jnp.float32), precision=highest_value)
    logits = jnp.einsum("tasc,c->tas", features, hyper, precision=highest_value)
    losses = jax.nn.softplus(logits) - truth * logits
    return jnp.sum(losses) * live_flag * 0.25


def on_device(
    embed,
    coords,
    targets,
    counts,
    labels,
    type_embed,
    fourier,
    wq_t,
    wk_t,
    wv_t,
    wo_t,
    wq_i,
    wk_i,
    wv_i,
    wo_i,
    gain_one,
    gain_two,
    gain_three,
    up_one,
    second_upsample_weight,
    hyper_one,
    hyper_two,
):
    prompt_count = lax.axis_size("prompt")
    enc_count = lax.axis_size("enc")
    prompt_place = lax.axis_index("prompt")
    enc_place = lax.axis_index("enc")
    block_rows = embed.shape[0]
    slot_count = coords.shape[0]
    head_scale = HD ** (-0.5)
    image = lax.all_gather(embed, "prompt", axis=0, tiled=True)
    image_float = image.astype(jnp.float32)
    key_image = jnp.dot(image, wk_t, preferred_element_type=jnp.float32)
    value_image = jnp.dot(image, wv_t, preferred_element_type=jnp.float32)
    query_image = jnp.dot(image, wq_i, preferred_element_type=jnp.float32)
    local_rows = image.shape[0]
    pixel_all = token_pixel_scores(labels).reshape(prompt_count, enc_count, block_rows, 4, 4)
    own_pixels = lax.dynamic_index_in_dim(pixel_all, enc_place, axis=1, keepdims=False).reshape(
        local_rows, 4, 4
    )
    own_count = jnp.take(counts, prompt_place)
    live_flags = (jnp.arange(slot_count, dtype=jnp.int32) < own_count).astype(jnp.float32)
    tokens_zero = prompt_tokens(coords, type_embed, fourier)
    prompt_number = tokens_zero.shape[0]
    flat_tokens = tokens_zero.reshape(prompt_number * 4, -1)
    queries = jnp.dot(flat_tokens, wq_t.astype(jnp.float32), precision=highest_value).reshape(
        -1, HEADS, HD
    )
    key_heads = key_image.reshape(local_rows, HEADS, HD)
    value_heads = value_image.reshape(local_rows, HEADS, HD)
    scores = jnp.einsum("rhd,jhd->rhj", queries, key_heads, precision=highest_value) * head_scale
    local_top = jnp.max(scores, axis=-1)
    shifted = jnp.exp(scores - local_top[..., None])
    local_total = jnp.sum(shifted, axis=-1)
    local_accum = jnp.einsum("rhj,jhd->rhd", shifted, value_heads, precision=highest_value)
    global_top, global_total, global_accum = joined(
        (local_top, local_total, local_accum), "enc", combine_parts
    )
    gathered = global_accum / global_total[..., None]
    wo_t_float = wo_t.astype(jnp.float32)
    update = jnp.dot(gathered.reshape(prompt_number * 4, -1), wo_t_float, precision=highest_value)

    def token_norm(values):
        return layer_norm(values, gain_one)

    tokens_one, norm_pull = jax.vjp(token_norm, flat_tokens + update)
    side_weights = (
        wk_i,
        wv_i,
        wo_i,
        gain_two,
        up_one,
        gain_three,
        second_upsample_weight,
        hyper_one,
        hyper_two,
    )

    def single_prompt(carry, inputs):
        tokens_row, target, live_flag = inputs
        truth = (own_pixels == target).astype(jnp.float32)

        def loss_of(query_arg, image_arg, tokens_arg):
            return image_side(query_arg, image_arg, tokens_arg, truth, live_flag, side_weights)

        _, pullback = jax.vjp(loss_of, query_image, image_float, tokens_row)
        d_query, d_image, d_tokens = pullback(jnp.ones((), jnp.float32))
        return ((carry[0] + d_query, carry[1] + d_image), d_tokens)

    initial = (jnp.zeros_like(query_image), jnp.zeros_like(image_float))
    sums, token_parts = lax.scan(
        single_prompt, initial, (tokens_one.reshape(prompt_number, 4, -1), targets, live_flags)
    )
    query_grad, image_grad = sums
    token_grad = lax.psum(token_parts, "enc")
    (d_residual,) = norm_pull(token_grad.reshape(prompt_number * 4, -1))
    d_gathered = jnp.dot(d_residual, wo_t_float.T, precision=highest_value).reshape(-1, HEADS, HD)
    probs = jnp.exp(scores - global_top[..., None]) / global_total[..., None]
    d_probs = jnp.einsum("rhd,jhd->rhj", d_gathered, value_heads, precision=highest_value)
    delta_term = jnp.sum(d_gathered * gathered, axis=-1)
    d_scores = probs * (d_probs - delta_term[..., None]) * head_scale
    key_grad = jnp.einsum("rhj,rhd->jhd", d_scores, queries, precision=highest_value).reshape(
        local_rows, -1
    )
    value_grad = jnp.einsum("rhj,rhd->jhd", probs, d_gathered, precision=highest_value).reshape(
        local_rows, -1
    )
    wq_i_float = wq_i.astype(jnp.float32)
    wk_t_float = wk_t.astype(jnp.float32)
    wv_t_float = wv_t.astype(jnp.float32)
    result = image_grad
    result = result + jnp.dot(query_grad, wq_i_float.T, precision=highest_value)
    result = result + jnp.dot(key_grad, wk_t_float.T, precision=highest_value)
    result = result + jnp.dot(value_grad, wv_t_float.T, precision=highest_value)
    summed = lax.psum(result, "prompt")
    grad_embed = lax.dynamic_slice_in_dim(summed, prompt_place * block_rows, block_rows, 0)
    return grad_embed


def solution(mesh):
    in_specs = (
        P(("groups", "prompt", "enc"), None),
        P(("groups", "prompt"), None),
        P(("groups", "prompt")),
        P(),
        P("groups", None),
        P(),
        P(),
        P(),
        P(),
        P(),
        P(),
        P(),
        P(),
        P(),
        P(),
        P(),
        P(),
        P(),
        P(),
        P(),
        P(),
        P(),
    )
    out_specs = P(("groups", "prompt", "enc"), None)
    return jax.shard_map(
        on_device, mesh=mesh, in_specs=in_specs, out_specs=out_specs, check_vma=False
    )
```

profile of v0, /device:TPU:0, one launch (start us, length us, event | category | flops | bytes accessed | tf_op | source)
XLA Modules:
  0.0 566.2 jit_solution(3963014833679820841)
XLA Ops:
  12.3 17.4 %all_gather.21 = bf16[1024,256]{0,1:T(8,128)(2,1)S(1)} all-gather(bf16[256,256]{0,1:T(8,128)(2,1)S(1)} %copy.50), channel_id=1, replica_groups=mesh['groups'=2,'prompt'=4,'enc'=4] {'prompt'}, dimensions={0}, use_global_device_ids=true | all-gather | bytes 655360 | tf_op jit(solution)/shard_map/all_gather | solution.py:141
  33.9 7.2 %all-gather.2 = f32[128,8,16]{2,1,0:T(8,128)S(1)} all-gather(f32[32,8,16]{2,1,0:T(8,128)S(1)} %copy.52), channel_id=4, replica_groups=mesh['groups'=2,'prompt'=4,'enc'=4] {'enc'}, dimensions={0}, use_global_device_ids=true | all-gather | bytes 81920 | tf_op jit(solution)/shard_map/all_gather | solution.py:15
  41.4 5.2 all-gather.4
  46.6 5.2 all-gather.3
  55.4 27.0 %reshape.331 = s32[64,2,2,64,2,2]{5,4,3,2,1,0:T(2,128)} reshape(s32[256,256]{1,0:T(8,128)S(1)} %copy-done.55) | data formatting | bytes 524288 | tf_op jit(solution)/shard_map/reshape | solution.py:46
  82.4 20.9 %copy.55 = s32[64,64,2,2,2,2]{1,0,5,4,3,2:T(8,128)S(1)} copy(s32[64,64,2,2,2,2]{5,3,1,4,2,0:T(2,128)} %bitcast.446) | data formatting | bytes 524288 | tf_op jit(solution)/shard_map/transpose | solution.py:47
  105.7 374.7 %while.36 = (s32[]{:T(128)}, f32[1024,128]{0,1:T(8,128)}, f32[1024,256]{0,1:T(8,128)}, f32[8,4,256]{2,1,0:T(4,128)}, f32[8,4,256]{2,1,0:T(4,128)}, /*index=5*/bf...) while((s32[]{:T(128)}, f32[1024,128]{0,1:T(8,128)}, ...), condition=%wide.region_18.19_spmd.clone, body=%wide.region_6.18_spmd.clone.sunk | while | flops 692868864 | bytes 118107712 | solution.py:201
  112.7 3.8 fusion.345
  116.6 5.5 multiply_multiply_fusion.19
  123.1 1.9 fusion.346
  129.5 2.7 fusion.348
  132.2 3.6 multiply_reduce_fusion.13
  148.7 1.9 fusion.352
  158.6 3.8 fusion.345
  162.5 5.5 multiply_multiply_fusion.19
  169.0 1.9 fusion.346
  175.4 2.7 fusion.348
  178.0 3.6 multiply_reduce_fusion.13
  194.6 1.9 fusion.352
  196.5 1.9 bitcast_add_fusion.2
  205.6 3.8 fusion.345
  209.4 5.5 multiply_multiply_fusion.19
  216.0 1.9 fusion.346
  222.3 2.7 fusion.348
  225.0 3.6 multiply_reduce_fusion.13
  241.6 1.9 fusion.352
  243.5 1.9 bitcast_add_fusion.2
  252.5 3.8 fusion.345
  256.3 5.5 multiply_multiply_fusion.19
  262.9 1.9 fusion.346
  269.3 2.7 fusion.348
  271.9 3.6 multiply_reduce_fusion.13
  288.5 1.9 fusion.352
  290.4 1.9 bitcast_add_fusion.2
  299.4 3.8 fusion.345
  303.3 5.5 multiply_multiply_fusion.19
  309.9 1.9 fusion.346
  316.2 2.7 fusion.348
  318.9 3.6 multiply_reduce_fusion.13
  335.5 1.9 fusion.352
  337.4 1.9 bitcast_add_fusion.2
  346.4 3.8 fusion.345
  350.2 5.5 multiply_multiply_fusion.19
  356.8 1.9 fusion.346
  363.2 2.7 fusion.348
  365.8 3.6 multiply_reduce_fusion.13
  382.4 1.9 fusion.352
  384.3 1.9 bitcast_add_fusion.2
  393.3 3.8 fusion.345
  397.2 5.5 multiply_multiply_fusion.19
  403.7 1.9 fusion.346
  410.1 2.7 fusion.348
  412.8 3.6 multiply_reduce_fusion.13
  429.4 1.9 fusion.352
  431.3 1.9 bitcast_add_fusion.2
  440.3 3.8 fusion.345
  444.1 5.5 multiply_multiply_fusion.19
  457.0 2.7 fusion.348
  459.7 3.6 multiply_reduce_fusion.13
  476.3 1.9 fusion.352
  478.2 1.9 bitcast_add_fusion.2
  481.2 10.9 %psum.14 = f32[32,256]{1,0:T(8,128)S(1)} all-reduce(f32[32,256]{1,0:T(8,128)S(1)} %reshape.333), channel_id=1, replica_groups=mesh['groups'=2,'prompt'=4,'enc'=4] {'enc'}, use_global_device_ids=true, to_apply=%region_19.20 | all-reduce | flops 8192 | bytes 65536 | tf_op jit(solution)/shard_map/psum | solution.py:205
  496.0 2.1 fusion.118
  504.3 53.4 %all-reduce.3.cloned.1.call-done = f32[1024,256]{1,0:T(8,128)} async-done(((f32[1024,256]{1,0:T(8,128)}), f32[1024,256]{1,0:T(8,128)}) %all-reduce.3.cloned.1.call-update) | async-done | bytes 1048592 | tf_op jit(solution)/shard_map/psum | solution.py:225
  (1268 shorter events, 225.0 us)
Async XLA Ops:
  6.5 98.0 %copy-start = (bf16[256,128]{1,0:T(8,128)(2,1)S(1)}, bf16[256,128]{1,0:T(8,128)(2,1)}, u32[]{:S(2)}) copy-start(bf16[256,128]{1,0:T(8,128)(2,1)} %param.37) | copy-start | bytes 196612
  6.5 23.2 %copy-start.57 = (bf16[256,128]{1,0:T(8,128)(2,1)S(1)}, bf16[256,128]{1,0:T(8,128)(2,1)}, u32[]{:S(2)}) copy-start(bf16[256,128]{1,0:T(8,128)(2,1)} %param.34) | copy-start | bytes 196612
  6.5 23.5 %copy-start.59 = (bf16[256,128]{1,0:T(8,128)(2,1)S(1)}, bf16[256,128]{1,0:T(8,128)(2,1)}, u32[]{:S(2)}) copy-start(bf16[256,128]{1,0:T(8,128)(2,1)} %param.35) | copy-start | bytes 196612
  6.5 551.2 %all-reduce.3.cloned.1.call-start = ((), (), s32[]{:S(2)}) async-start(), calls=%async_computation | async-start | bytes 2097152 | tf_op jit(solution)/shard_map/psum | solution.py:225
  33.8 18.3 %copy-start.56 = (bf16[128,256]{1,0:T(8,128)(2,1)S(1)}, bf16[128,256]{1,0:T(8,128)(2,1)}, u32[]{:S(2)}) copy-start(bf16[128,256]{1,0:T(8,128)(2,1)} %param.36) | copy-start | bytes 196612
  33.8 19.2 %copy-start.70 = (f32[256]{0:T(256)S(1)}, f32[256]{0:T(256)}, u32[]{:S(2)}) copy-start(f32[256]{0:T(256)} %param.41) | copy-start | bytes 3076
  33.8 19.9 %copy-start.74 = (s32[4]{0:T(128)S(1)}, s32[4]{0:T(128)}, u32[]{:S(2)}) copy-start(s32[4]{0:T(128)} %param.29) | copy-start | bytes 52
  33.8 21.6 %copy-start.55 = (s32[256,256]{1,0:T(8,128)S(1)}, s32[256,256]{1,0:T(8,128)}, u32[]{:S(2)}) copy-start(s32[256,256]{1,0:T(8,128)} %param.30) | copy-start | bytes 786436
  52.0 30.4 %copy-start.63 = (f32[32,8]{0,1:T(8,128)}, f32[32,8]{0,1:T(8,128)S(1)}, u32[]{:S(2)}) copy-start(f32[32,8]{0,1:T(8,128)S(1)} %get-tuple-element.283) | copy-start | bytes 3076
  52.0 30.4 %copy-start.65 = (f32[32,8]{0,1:T(8,128)}, f32[32,8]{0,1:T(8,128)S(1)}, u32[]{:S(2)}) copy-start(f32[32,8]{0,1:T(8,128)S(1)} %get-tuple-element.286) | copy-start | bytes 3076
  52.0 30.4 %copy-start.52 = (f32[32,8,16]{0,2,1:T(8,128)}, f32[32,8,16]{0,2,1:T(8,128)S(1)}, u32[]{:S(2)}) copy-start(f32[32,8,16]{0,2,1:T(8,128)S(1)} %broadcast_divide_fusion) | copy-start | bytes 49156
  52.4 30.0 %copy-start.71 = (f32[32]{0:T(128)}, f32[32]{0:T(128)S(1)}, u32[]{:S(2)}) copy-start(f32[32]{0:T(128)S(1)} %broadcast_multiply_fusion.3) | copy-start | bytes 388
  52.6 29.8 %copy-start.73 = (f32[32]{0:T(128)}, f32[32]{0:T(128)S(1)}, u32[]{:S(2)}) copy-start(f32[32]{0:T(128)S(1)} %multiply_reduce_fusion.6) | copy-start | bytes 388
  53.0 29.5 %copy-start.72 = (f32[32]{0:T(128)}, f32[32]{0:T(128)S(1)}, u32[]{:S(2)}) copy-start(f32[32]{0:T(128)S(1)} %fusion.146) | copy-start | bytes 388
  105.7 4.9 copy-start.7
  105.7 5.0 copy-start.22
  116.5 5.6 copy-start.5
  116.5 5.6 copy-start.18
  116.5 6.4 %copy-start.53 = (bf16[256,32]{0,1:T(8,128)(2,1)S(1)}, bf16[256,32]{0,1:T(8,128)(2,1)}, u32[]{:S(2)}) copy-start(bf16[256,32]{0,1:T(8,128)(2,1)} %get-tuple-element.825) | copy-start | bytes 49156 | tf_op jit(solution)/shard_map/while
  141.7 6.0 %copy-start.4 = (f32[1024,256]{0,1:T(8,128)S(1)}, f32[1024,256]{0,1:T(8,128)}, u32[]{:S(2)}) copy-start(f32[1024,256]{0,1:T(8,128)} %copy-done.3) | copy-start | bytes 3145732 | tf_op jit(solution)/shard_map/while
  151.6 4.9 copy-start.7
  151.6 4.9 copy-start.22
  162.4 5.6 copy-start.5
  162.4 5.6 copy-start.18
  162.4 6.4 %copy-start.53 = (bf16[256,32]{0,1:T(8,128)(2,1)S(1)}, bf16[256,32]{0,1:T(8,128)(2,1)}, u32[]{:S(2)}) copy-start(bf16[256,32]{0,1:T(8,128)(2,1)} %get-tuple-element.825) | copy-start | bytes 49156 | tf_op jit(solution)/shard_map/while
  187.5 6.0 %copy-start.4 = (f32[1024,256]{0,1:T(8,128)S(1)}, f32[1024,256]{0,1:T(8,128)}, u32[]{:S(2)}) copy-start(f32[1024,256]{0,1:T(8,128)} %copy-done.3) | copy-start | bytes 3145732 | tf_op jit(solution)/shard_map/while
  190.4 4.2 copy-start.40
  198.5 4.9 copy-start.7
  198.5 4.9 copy-start.22
  209.4 5.6 copy-start.5
  209.4 5.6 copy-start.18
  209.4 6.5 %copy-start.53 = (bf16[256,32]{0,1:T(8,128)(2,1)S(1)}, bf16[256,32]{0,1:T(8,128)(2,1)}, u32[]{:S(2)}) copy-start(bf16[256,32]{0,1:T(8,128)(2,1)} %get-tuple-element.825) | copy-start | bytes 49156 | tf_op jit(solution)/shard_map/while
  234.5 6.0 %copy-start.4 = (f32[1024,256]{0,1:T(8,128)S(1)}, f32[1024,256]{0,1:T(8,128)}, u32[]{:S(2)}) copy-start(f32[1024,256]{0,1:T(8,128)} %copy-done.3) | copy-start | bytes 3145732 | tf_op jit(solution)/shard_map/while
  245.5 4.9 copy-start.7
  245.5 4.9 copy-start.22
  256.3 5.6 copy-start.5
  256.3 5.6 copy-start.18
  256.3 6.5 %copy-start.53 = (bf16[256,32]{0,1:T(8,128)(2,1)S(1)}, bf16[256,32]{0,1:T(8,128)(2,1)}, u32[]{:S(2)}) copy-start(bf16[256,32]{0,1:T(8,128)(2,1)} %get-tuple-element.825) | copy-start | bytes 49156 | tf_op jit(solution)/shard_map/while
  281.5 6.0 %copy-start.4 = (f32[1024,256]{0,1:T(8,128)S(1)}, f32[1024,256]{0,1:T(8,128)}, u32[]{:S(2)}) copy-start(f32[1024,256]{0,1:T(8,128)} %copy-done.3) | copy-start | bytes 3145732 | tf_op jit(solution)/shard_map/while
  292.4 4.9 copy-start.7
  292.4 4.9 copy-start.22
  303.3 5.6 copy-start.5
  303.3 5.6 copy-start.18
  303.3 6.5 %copy-start.53 = (bf16[256,32]{0,1:T(8,128)(2,1)S(1)}, bf16[256,32]{0,1:T(8,128)(2,1)}, u32[]{:S(2)}) copy-start(bf16[256,32]{0,1:T(8,128)(2,1)} %get-tuple-element.825) | copy-start | bytes 49156 | tf_op jit(solution)/shard_map/while
  328.4 6.0 %copy-start.4 = (f32[1024,256]{0,1:T(8,128)S(1)}, f32[1024,256]{0,1:T(8,128)}, u32[]{:S(2)}) copy-start(f32[1024,256]{0,1:T(8,128)} %copy-done.3) | copy-start | bytes 3145732 | tf_op jit(solution)/shard_map/while
  339.3 4.9 copy-start.7
  339.4 4.9 copy-start.22
  350.2 5.6 copy-start.5
  350.2 5.6 copy-start.18
  350.2 6.5 %copy-start.53 = (bf16[256,32]{0,1:T(8,128)(2,1)S(1)}, bf16[256,32]{0,1:T(8,128)(2,1)}, u32[]{:S(2)}) copy-start(bf16[256,32]{0,1:T(8,128)(2,1)} %get-tuple-element.825) | copy-start | bytes 49156 | tf_op jit(solution)/shard_map/while
  375.3 6.0 %copy-start.4 = (f32[1024,256]{0,1:T(8,128)S(1)}, f32[1024,256]{0,1:T(8,128)}, u32[]{:S(2)}) copy-start(f32[1024,256]{0,1:T(8,128)} %copy-done.3) | copy-start | bytes 3145732 | tf_op jit(solution)/shard_map/while
  386.3 4.9 copy-start.7
  386.3 4.9 copy-start.22
  397.2 5.6 copy-start.5
  397.2 5.6 copy-start.18
  397.2 6.4 %copy-start.53 = (bf16[256,32]{0,1:T(8,128)(2,1)S(1)}, bf16[256,32]{0,1:T(8,128)(2,1)}, u32[]{:S(2)}) copy-start(bf16[256,32]{0,1:T(8,128)(2,1)} %get-tuple-element.825) | copy-start | bytes 49156 | tf_op jit(solution)/shard_map/while
  422.3 6.0 %copy-start.4 = (f32[1024,256]{0,1:T(8,128)S(1)}, f32[1024,256]{0,1:T(8,128)}, u32[]{:S(2)}) copy-start(f32[1024,256]{0,1:T(8,128)} %copy-done.3) | copy-start | bytes 3145732 | tf_op jit(solution)/shard_map/while
  425.2 4.2 copy-start.40
  433.2 4.9 copy-start.7
  433.3 4.9 copy-start.22
  444.1 5.6 copy-start.5
  444.1 5.6 copy-start.18
  444.1 6.4 %copy-start.53 = (bf16[256,32]{0,1:T(8,128)(2,1)S(1)}, bf16[256,32]{0,1:T(8,128)(2,1)}, u32[]{:S(2)}) copy-start(bf16[256,32]{0,1:T(8,128)(2,1)} %get-tuple-element.825) | copy-start | bytes 49156 | tf_op jit(solution)/shard_map/while
  469.2 6.0 %copy-start.4 = (f32[1024,256]{0,1:T(8,128)S(1)}, f32[1024,256]{0,1:T(8,128)}, u32[]{:S(2)}) copy-start(f32[1024,256]{0,1:T(8,128)} %copy-done.3) | copy-start | bytes 3145732 | tf_op jit(solution)/shard_map/while
  (357 other events, 860.2 us)
Sparse Core Ops, SparseCore 0:
  504.4 53.2 all-reduce.2
where the time goes:
time: 573 us; the launch traced here: 566 us
  matrix products  223 us (39%)
  other arithmetic  124 us (22%)
  local copies, waits for them, and re-layouts  95 us (17%)
  waiting for transfers between devices  53.4 us (9%)
  blocking collectives  45.8 us (8%)
  between operations  14.6 us (3%)
  loops' own time  11.1 us (2%)
    dot_general x16, matrix products, image_side(): jnp.einsum('oij,jp->oip', first_activation, second_upsample_weight, prefe...  59.2 us
    psum x1, waiting for transfers between devices, on_device(): summed = lax.psum(result, 'prompt')  53.4 us
    mul x8, other arithmetic, image_side(): jax.nn.gelu(second_result, approximate=False).reshape(row_count, 4, 4, -1)  44.4 us
    dot_general x16, matrix products, image_side(): logits = jnp.einsum('tasc,c->tas', features, hyper, precision=highest_value)  28.8 us
    reshape x1, local copies, waits for them, and re-layouts, token_pixel_scores(): grid_view = labels.reshape(side, 2, 2, side, 2, 2)  27 us
    dot_general x24, matrix products, image_side(): jnp.einsum('jhd,rhd->jhr', query_image.reshape(row_count, HEADS, HD), tok...  24.1 us
    dot_general x16, matrix products, image_side(): jnp.dot(tokens_one, wk_i.astype(jnp.float32), precision=highest_value)  23 us
    add x16, other arithmetic, single_prompt(): return ((carry[0] + d_query, carry[1] + d_image), d_tokens)  22.7 us
  transfers between devices with their start and end apart: 1, of which 1 were waited for; matrix products, arithmetic and copies ran while one was open for 0% of the time, Pallas kernels for 0%

commit v1 on v0

--- a/solution.py
+++ b/solution.py
@@ -222,7 +222,7 @@
     result = result + jnp.dot(query_grad, wq_i_float.T, precision=highest_value)
     result = result + jnp.dot(key_grad, wk_t_float.T, precision=highest_value)
     result = result + jnp.dot(value_grad, wv_t_float.T, precision=highest_value)
-    summed = lax.psum(result, "prompt")
+    summed = jnp.sum(lax.all_gather(result, "prompt"), axis=0)
     grad_embed = lax.dynamic_slice_in_dim(summed, prompt_place * block_rows, block_rows, 0)
     return grad_embed
 

time: 573 us -> 603 us (1.052)
  waiting for transfers between devices: 53.4 us -> 82.4 us
    all_gather x0 -> x1, waiting for transfers between devices: none -> 82.4 us  [on_device(): summed = jnp.sum(lax.all_gather(result, 'prompt'), axis=0)]
    psum x1 -> x0, waiting for transfers between devices: 53.4 us -> none  [on_device(): summed = lax.psum(result, 'prompt')]
where the time goes in v1:
time: 603 us; the launch traced here: 597 us
  matrix products  223 us (37%)
  other arithmetic  126 us (21%)
  local copies, waits for them, and re-layouts  94 us (16%)
  waiting for transfers between devices  82.4 us (14%)
  blocking collectives  45.8 us (8%)
  between operations  14.6 us (2%)
  loops' own time  11.1 us (2%)
    all_gather x1, waiting for transfers between devices, on_device(): summed = jnp.sum(lax.all_gather(result, 'prompt'), axis=0)  82.4 us
    dot_general x16, matrix products, image_side(): jnp.einsum('oij,jp->oip', first_activation, second_upsample_weight, prefe...  59.2 us
    mul x8, other arithmetic, image_side(): jax.nn.gelu(second_result, approximate=False).reshape(row_count, 4, 4, -1)  44.4 us
    dot_general x16, matrix products, image_side(): logits = jnp.einsum('tasc,c->tas', features, hyper, precision=highest_value)  28.8 us
    reshape x1, local copies, waits for them, and re-layouts, token_pixel_scores(): grid_view = labels.reshape(side, 2, 2, side, 2, 2)  27 us
    dot_general x24, matrix products, image_side(): jnp.einsum('jhd,rhd->jhr', query_image.reshape(row_count, HEADS, HD), tok...  24.1 us
    dot_general x16, matrix products, image_side(): jnp.dot(tokens_one, wk_i.astype(jnp.float32), precision=highest_value)  23 us
    add x16, other arithmetic, single_prompt(): return ((carry[0] + d_query, carry[1] + d_image), d_tokens)  22.7 us
  transfers between devices with their start and end apart: 1, of which 1 were waited for; matrix products, arithmetic and copies ran while one was open for 0% of the time, Pallas kernels for 0%

profile of v1, /device:TPU:0, one launch (start us, length us, event | category | flops | bytes accessed | tf_op | source)
XLA Modules:
  0.0 596.9 jit_solution(15863343824143602529)
XLA Ops:
  12.3 17.4 %all_gather.27 = bf16[1024,256]{0,1:T(8,128)(2,1)S(1)} all-gather(bf16[256,256]{0,1:T(8,128)(2,1)S(1)} %copy.50), channel_id=1, replica_groups=mesh['groups'=2,'prompt'=4,'enc'=4] {'prompt'}, dimensions={0}, use_global_device_ids=true | all-gather | bytes 655360 | tf_op jit(solution)/shard_map/all_gather | solution.py:141
  33.9 7.2 %all-gather.2 = f32[128,8,16]{2,1,0:T(8,128)S(1)} all-gather(f32[32,8,16]{2,1,0:T(8,128)S(1)} %copy.52), channel_id=4, replica_groups=mesh['groups'=2,'prompt'=4,'enc'=4] {'enc'}, dimensions={0}, use_global_device_ids=true | all-gather | bytes 81920 | tf_op jit(solution)/shard_map/all_gather | solution.py:15
  41.4 5.2 all-gather.5
  46.6 5.2 all-gather.4
  55.4 27.0 %reshape.331 = s32[64,2,2,64,2,2]{5,4,3,2,1,0:T(2,128)} reshape(s32[256,256]{1,0:T(8,128)S(1)} %copy-done.55) | data formatting | bytes 524288 | tf_op jit(solution)/shard_map/reshape | solution.py:46
  82.4 20.9 %copy.55 = s32[64,64,2,2,2,2]{1,0,5,4,3,2:T(8,128)S(1)} copy(s32[64,64,2,2,2,2]{5,3,1,4,2,0:T(2,128)} %bitcast.447) | data formatting | bytes 524288 | tf_op jit(solution)/shard_map/transpose | solution.py:47
  105.7 374.7 %while.36 = (s32[]{:T(128)}, f32[1024,128]{0,1:T(8,128)}, f32[1024,256]{0,1:T(8,128)}, f32[8,4,256]{2,1,0:T(4,128)}, f32[8,4,256]{2,1,0:T(4,128)}, /*index=5*/bf...) while((s32[]{:T(128)}, f32[1024,128]{0,1:T(8,128)}, ...), condition=%wide.region_18.19_spmd.clone, body=%wide.region_6.18_spmd.clone.sunk | while | flops 692868864 | bytes 118107712 | solution.py:201
  112.7 3.8 fusion.345
  116.6 5.5 multiply_multiply_fusion.19
  123.1 1.9 fusion.346
  129.5 2.7 fusion.348
  132.2 3.6 multiply_reduce_fusion.13
  148.7 1.9 fusion.352
  158.6 3.8 fusion.345
  162.5 5.5 multiply_multiply_fusion.19
  169.0 1.9 fusion.346
  175.4 2.7 fusion.348
  178.0 3.6 multiply_reduce_fusion.13
  194.6 1.9 fusion.352
  196.5 1.9 bitcast_add_fusion.2
  205.6 3.8 fusion.345
  209.4 5.5 multiply_multiply_fusion.19
  216.0 1.9 fusion.346
  222.3 2.7 fusion.348
  225.0 3.6 multiply_reduce_fusion.13
  241.6 1.9 fusion.352
  243.5 1.9 bitcast_add_fusion.2
  252.5 3.8 fusion.345
  256.3 5.5 multiply_multiply_fusion.19
  269.3 2.7 fusion.348
  271.9 3.6 multiply_reduce_fusion.13
  288.5 1.9 fusion.352
  290.4 1.9 bitcast_add_fusion.2
  299.4 3.8 fusion.345
  303.3 5.5 multiply_multiply_fusion.19
  309.9 1.9 fusion.346
  316.2 2.7 fusion.348
  318.9 3.6 multiply_reduce_fusion.13
  335.5 1.9 fusion.352
  337.4 1.9 bitcast_add_fusion.2
  346.4 3.8 fusion.345
  350.2 5.5 multiply_multiply_fusion.19
  356.8 1.9 fusion.346
  363.2 2.7 fusion.348
  365.8 3.6 multiply_reduce_fusion.13
  382.4 1.9 fusion.352
  384.3 1.9 bitcast_add_fusion.2
  393.3 3.8 fusion.345
  397.2 5.5 multiply_multiply_fusion.19
  403.7 1.9 fusion.346
  410.1 2.7 fusion.348
  412.8 3.6 multiply_reduce_fusion.13
  429.4 1.9 fusion.352
  431.3 1.9 bitcast_add_fusion.2
  440.3 3.8 fusion.345
  444.1 5.5 multiply_multiply_fusion.19
  457.0 2.7 fusion.348
  459.7 3.6 multiply_reduce_fusion.13
  476.3 1.9 fusion.352
  478.2 1.9 bitcast_add_fusion.2
  481.2 10.9 %psum.7 = f32[32,256]{1,0:T(8,128)S(1)} all-reduce(f32[32,256]{1,0:T(8,128)S(1)} %reshape.333), channel_id=1, replica_groups=mesh['groups'=2,'prompt'=4,'enc'=4] {'enc'}, use_global_device_ids=true, to_apply=%region_19.20 | all-reduce | flops 8192 | bytes 65536 | tf_op jit(solution)/shard_map/psum | solution.py:205
  496.0 2.1 fusion.118
  504.4 82.4 %all-gather.8.cloned.1.call-done = f32[4096,256]{1,0:T(8,128)} async-done(((f32[1024,256]{1,0:T(8,128)}), f32[4096,256]{1,0:T(8,128)}) %all-gather.8.cloned.1.call-update) | async-done | bytes 4194320 | tf_op jit(solution)/shard_map/all_gather | solution.py:225
  586.7 2.6 reduce_sum.175
  (1269 shorter events, 226.0 us)
Async XLA Ops:
  6.5 98.0 %copy-start = (bf16[256,128]{1,0:T(8,128)(2,1)S(1)}, bf16[256,128]{1,0:T(8,128)(2,1)}, u32[]{:S(2)}) copy-start(bf16[256,128]{1,0:T(8,128)(2,1)} %param.37) | copy-start | bytes 196612
  6.5 23.2 %copy-start.57 = (bf16[256,128]{1,0:T(8,128)(2,1)S(1)}, bf16[256,128]{1,0:T(8,128)(2,1)}, u32[]{:S(2)}) copy-start(bf16[256,128]{1,0:T(8,128)(2,1)} %param.34) | copy-start | bytes 196612
  6.5 23.5 %copy-start.59 = (bf16[256,128]{1,0:T(8,128)(2,1)S(1)}, bf16[256,128]{1,0:T(8,128)(2,1)}, u32[]{:S(2)}) copy-start(bf16[256,128]{1,0:T(8,128)(2,1)} %param.35) | copy-start | bytes 196612
  6.5 580.2 %all-gather.8.cloned.1.call-start = ((), (), s32[]{:S(2)}) async-start(), calls=%async_computation | async-start | bytes 5242880 | tf_op jit(solution)/shard_map/all_gather | solution.py:225
  33.8 18.3 %copy-start.56 = (bf16[128,256]{1,0:T(8,128)(2,1)S(1)}, bf16[128,256]{1,0:T(8,128)(2,1)}, u32[]{:S(2)}) copy-start(bf16[128,256]{1,0:T(8,128)(2,1)} %param.36) | copy-start | bytes 196612
  33.8 19.2 %copy-start.70 = (f32[256]{0:T(256)S(1)}, f32[256]{0:T(256)}, u32[]{:S(2)}) copy-start(f32[256]{0:T(256)} %param.41) | copy-start | bytes 3076
  33.8 19.9 %copy-start.74 = (s32[4]{0:T(128)S(1)}, s32[4]{0:T(128)}, u32[]{:S(2)}) copy-start(s32[4]{0:T(128)} %param.29) | copy-start | bytes 52
  33.8 21.6 %copy-start.55 = (s32[256,256]{1,0:T(8,128)S(1)}, s32[256,256]{1,0:T(8,128)}, u32[]{:S(2)}) copy-start(s32[256,256]{1,0:T(8,128)} %param.30) | copy-start | bytes 786436
  52.0 30.4 %copy-start.63 = (f32[32,8]{0,1:T(8,128)}, f32[32,8]{0,1:T(8,128)S(1)}, u32[]{:S(2)}) copy-start(f32[32,8]{0,1:T(8,128)S(1)} %get-tuple-element.283) | copy-start | bytes 3076
  52.0 30.4 %copy-start.65 = (f32[32,8]{0,1:T(8,128)}, f32[32,8]{0,1:T(8,128)S(1)}, u32[]{:S(2)}) copy-start(f32[32,8]{0,1:T(8,128)S(1)} %get-tuple-element.286) | copy-start | bytes 3076
  52.0 30.4 %copy-start.52 = (f32[32,8,16]{0,2,1:T(8,128)}, f32[32,8,16]{0,2,1:T(8,128)S(1)}, u32[]{:S(2)}) copy-start(f32[32,8,16]{0,2,1:T(8,128)S(1)} %broadcast_divide_fusion) | copy-start | bytes 49156
  52.4 30.0 %copy-start.71 = (f32[32]{0:T(128)}, f32[32]{0:T(128)S(1)}, u32[]{:S(2)}) copy-start(f32[32]{0:T(128)S(1)} %broadcast_multiply_fusion.3) | copy-start | bytes 388
  52.6 29.8 %copy-start.73 = (f32[32]{0:T(128)}, f32[32]{0:T(128)S(1)}, u32[]{:S(2)}) copy-start(f32[32]{0:T(128)S(1)} %multiply_reduce_fusion.6) | copy-start | bytes 388
  53.0 29.5 %copy-start.72 = (f32[32]{0:T(128)}, f32[32]{0:T(128)S(1)}, u32[]{:S(2)}) copy-start(f32[32]{0:T(128)S(1)} %fusion.146) | copy-start | bytes 388
  105.7 4.9 copy-start.7
  105.7 5.0 copy-start.22
  116.5 5.6 copy-start.5
  116.5 5.6 copy-start.18
  116.5 6.4 %copy-start.53 = (bf16[256,32]{0,1:T(8,128)(2,1)S(1)}, bf16[256,32]{0,1:T(8,128)(2,1)}, u32[]{:S(2)}) copy-start(bf16[256,32]{0,1:T(8,128)(2,1)} %get-tuple-element.825) | copy-start | bytes 49156 | tf_op jit(solution)/shard_map/while
  141.7 6.0 %copy-start.4 = (f32[1024,256]{0,1:T(8,128)S(1)}, f32[1024,256]{0,1:T(8,128)}, u32[]{:S(2)}) copy-start(f32[1024,256]{0,1:T(8,128)} %copy-done.3) | copy-start | bytes 3145732 | tf_op jit(solution)/shard_map/while
  151.6 4.9 copy-start.7
  151.6 4.9 copy-start.22
  162.4 5.6 copy-start.5
  162.4 5.6 copy-start.18
  162.4 6.4 %copy-start.53 = (bf16[256,32]{0,1:T(8,128)(2,1)S(1)}, bf16[256,32]{0,1:T(8,128)(2,1)}, u32[]{:S(2)}) copy-start(bf16[256,32]{0,1:T(8,128)(2,1)} %get-tuple-element.825) | copy-start | bytes 49156 | tf_op jit(solution)/shard_map/while
  187.5 6.0 %copy-start.4 = (f32[1024,256]{0,1:T(8,128)S(1)}, f32[1024,256]{0,1:T(8,128)}, u32[]{:S(2)}) copy-start(f32[1024,256]{0,1:T(8,128)} %copy-done.3) | copy-start | bytes 3145732 | tf_op jit(solution)/shard_map/while
  190.4 4.2 copy-start.40
  198.5 4.9 copy-start.7
  198.5 4.9 copy-start.22
  209.4 5.6 copy-start.5
  209.4 5.6 copy-start.18
  209.4 6.5 %copy-start.53 = (bf16[256,32]{0,1:T(8,128)(2,1)S(1)}, bf16[256,32]{0,1:T(8,128)(2,1)}, u32[]{:S(2)}) copy-start(bf16[256,32]{0,1:T(8,128)(2,1)} %get-tuple-element.825) | copy-start | bytes 49156 | tf_op jit(solution)/shard_map/while
  234.5 6.0 %copy-start.4 = (f32[1024,256]{0,1:T(8,128)S(1)}, f32[1024,256]{0,1:T(8,128)}, u32[]{:S(2)}) copy-start(f32[1024,256]{0,1:T(8,128)} %copy-done.3) | copy-start | bytes 3145732 | tf_op jit(solution)/shard_map/while
  245.5 4.9 copy-start.7
  245.5 4.9 copy-start.22
  256.3 5.6 copy-start.5
  256.3 5.6 copy-start.18
  256.3 6.5 %copy-start.53 = (bf16[256,32]{0,1:T(8,128)(2,1)S(1)}, bf16[256,32]{0,1:T(8,128)(2,1)}, u32[]{:S(2)}) copy-start(bf16[256,32]{0,1:T(8,128)(2,1)} %get-tuple-element.825) | copy-start | bytes 49156 | tf_op jit(solution)/shard_map/while
  281.5 6.0 %copy-start.4 = (f32[1024,256]{0,1:T(8,128)S(1)}, f32[1024,256]{0,1:T(8,128)}, u32[]{:S(2)}) copy-start(f32[1024,256]{0,1:T(8,128)} %copy-done.3) | copy-start | bytes 3145732 | tf_op jit(solution)/shard_map/while
  292.4 4.9 copy-start.7
  292.4 4.9 copy-start.22
  303.3 5.6 copy-start.5
  303.3 5.6 copy-start.18
  303.3 6.5 %copy-start.53 = (bf16[256,32]{0,1:T(8,128)(2,1)S(1)}, bf16[256,32]{0,1:T(8,128)(2,1)}, u32[]{:S(2)}) copy-start(bf16[256,32]{0,1:T(8,128)(2,1)} %get-tuple-element.825) | copy-start | bytes 49156 | tf_op jit(solution)/shard_map/while
  328.4 6.0 %copy-start.4 = (f32[1024,256]{0,1:T(8,128)S(1)}, f32[1024,256]{0,1:T(8,128)}, u32[]{:S(2)}) copy-start(f32[1024,256]{0,1:T(8,128)} %copy-done.3) | copy-start | bytes 3145732 | tf_op jit(solution)/shard_map/while
  339.3 4.9 copy-start.7
  339.4 4.9 copy-start.22
  350.2 5.6 copy-start.5
  350.2 5.6 copy-start.18
  350.2 6.5 %copy-start.53 = (bf16[256,32]{0,1:T(8,128)(2,1)S(1)}, bf16[256,32]{0,1:T(8,128)(2,1)}, u32[]{:S(2)}) copy-start(bf16[256,32]{0,1:T(8,128)(2,1)} %get-tuple-element.825) | copy-start | bytes 49156 | tf_op jit(solution)/shard_map/while
  375.3 6.0 %copy-start.4 = (f32[1024,256]{0,1:T(8,128)S(1)}, f32[1024,256]{0,1:T(8,128)}, u32[]{:S(2)}) copy-start(f32[1024,256]{0,1:T(8,128)} %copy-done.3) | copy-start | bytes 3145732 | tf_op jit(solution)/shard_map/while
  386.3 4.9 copy-start.7
  386.3 4.9 copy-start.22
  397.2 5.6 copy-start.5
  397.2 5.6 copy-start.18
  397.2 6.4 %copy-start.53 = (bf16[256,32]{0,1:T(8,128)(2,1)S(1)}, bf16[256,32]{0,1:T(8,128)(2,1)}, u32[]{:S(2)}) copy-start(bf16[256,32]{0,1:T(8,128)(2,1)} %get-tuple-element.825) | copy-start | bytes 49156 | tf_op jit(solution)/shard_map/while
  422.3 6.0 %copy-start.4 = (f32[1024,256]{0,1:T(8,128)S(1)}, f32[1024,256]{0,1:T(8,128)}, u32[]{:S(2)}) copy-start(f32[1024,256]{0,1:T(8,128)} %copy-done.3) | copy-start | bytes 3145732 | tf_op jit(solution)/shard_map/while
  425.2 4.2 copy-start.40
  433.2 4.9 copy-start.7
  433.3 4.9 copy-start.22
  444.1 5.6 copy-start.5
  444.1 5.6 copy-start.18
  444.1 6.4 %copy-start.53 = (bf16[256,32]{0,1:T(8,128)(2,1)S(1)}, bf16[256,32]{0,1:T(8,128)(2,1)}, u32[]{:S(2)}) copy-start(bf16[256,32]{0,1:T(8,128)(2,1)} %get-tuple-element.825) | copy-start | bytes 49156 | tf_op jit(solution)/shard_map/while
  469.2 6.0 %copy-start.4 = (f32[1024,256]{0,1:T(8,128)S(1)}, f32[1024,256]{0,1:T(8,128)}, u32[]{:S(2)}) copy-start(f32[1024,256]{0,1:T(8,128)} %copy-done.3) | copy-start | bytes 3145732 | tf_op jit(solution)/shard_map/while
  (357 other events, 860.2 us)
Sparse Core Ops, SparseCore 0:
  504.5 82.2 all-gather.7
